TPU v7x, 256 devices: a whole 4x4x8 slice. The times are simulated.
256 devices in a mesh: leaf: 2 (over core), row: 8 (over z), col: 16 (over y, x).
Axes of the slice: x: 4, y: 4, z: 8, core: 2. Of those that a mesh axis runs over, the one named last changes fastest.
Arguments:
- front: float32 [2, 8, 8, 128, 4, 16, 128], P('leaf', None, 'row', None, None, 'col'), as said below
- parent: float32 [4, 2, 8, 128, 4, 16, 128], P(None, 'leaf', 'row', None, None, 'col'), may hold values from -0.2 to 0.2
- tile_map: int32 [2, 56], replicated, may hold values from 0 to 63, as said below
- col_shift: int32 [4], replicated, may hold values from 0 to 7
Outputs:
- factored: float32 [2, 8, 8, 128, 4, 16, 128], P('leaf', None, 'row', None, None, 'col')
- new_parent: float32 [4, 2, 8, 128, 4, 16, 128], P(None, 'leaf', 'row', None, None, 'col')
Inputs may be any that keep to these rules, and one draw needn't show every extreme that they name: For each leaf the 8192 x 8192 matrix read from front is symmetric positive definite. Entry [l, e] names the parent tile joined by tile 8 + e of child l; no row repeats a value. The parent tile q = tile_map[l, e] has (q mod 16 + col_shift[q // 16]) mod 16 equal to (8 + e) mod 16. Among the tiles of one child whose indices are equal mod 8, at most 1 have parent tiles equal mod 16.
All inputs are finite; a program needn't handle non-finite values.
Results may differ from a plain program's by a relative error of at most 0.0001.
Values sent between devices are 32-bit elements; how exact they have to be, the bound alone decides.
No kernel may reach another device: no remote copies, remote signals or barrier semaphores. Data moves between devices by JAX's collectives and lax.ppermute only.
A program may use at most 128 MiB of HBM per device.

v0:
```python
import jax
import jax.numpy as jnp
from jax import lax
from jax.sharding import PartitionSpec as P

TILE = 128
PB = 512
PANELS = 2
NPIV = 1024
HIGHEST = lax.Precision.HIGHEST


def spread(value, axis, source):
    kept = jnp.where(lax.axis_index(axis) == source, value, 0).astype(value.dtype)
    return lax.psum(kept, axis)


def update_slots(working, next_rows, column_factor, slot_low, slot_high):
    product = jnp.einsum(
        "atp,bsp->atbs",
        next_rows,
        column_factor,
        precision=HIGHEST,
        preferred_element_type=jnp.float32,
    )
    return working.at[:, :, slot_low:slot_high, :].add(-product)


def tall_cholesky(diagonal_block, below_rows):
    size = diagonal_block.shape[0]
    remaining = diagonal_block
    eye = jnp.eye(TILE, dtype=jnp.float32)
    diag_columns = []
    inverses = []
    for step in range(size // TILE):
        low = step * TILE
        left = size - low - TILE
        pivot = remaining[:TILE, :TILE]
        pivot_factor = jnp.linalg.cholesky(pivot)
        pivot_inverse = lax.linalg.triangular_solve(pivot_factor, eye, left_side=True, lower=True)
        inverses.append(pivot_inverse)
        parts = [jnp.zeros((low, TILE), jnp.float32), pivot_factor]
        if left:
            solved = jnp.dot(
                remaining[TILE:, :TILE],
                pivot_inverse.T,
                precision=HIGHEST,
                preferred_element_type=jnp.float32,
            )
            parts.append(solved)
            update = jnp.dot(
                solved, solved.T, precision=HIGHEST, preferred_element_type=jnp.float32
            )
            remaining = remaining[TILE:, TILE:] - update
        diag_columns.append(jnp.concatenate(parts, axis=0))
    lower_factor = jnp.concatenate(diag_columns, axis=1)
    rest = below_rows
    below_columns = []
    for step in range(size // TILE):
        low = step * TILE
        solved = jnp.dot(
            rest[:, :TILE], inverses[step].T, precision=HIGHEST, preferred_element_type=jnp.float32
        )
        below_columns.append(solved)
        if low + TILE < size:
            update = jnp.dot(
                solved,
                lower_factor[low + TILE :, low : low + TILE].T,
                precision=HIGHEST,
                preferred_element_type=jnp.float32,
            )
            rest = rest[:, TILE:] - update
    return (lower_factor, jnp.concatenate(below_columns, axis=1))


def per_device(front, parent, tile_map, col_shift):
    leaf_count = lax.axis_size("leaf")
    row_count = lax.axis_size("row")
    col_count = lax.axis_size("col")
    leaf_index = lax.axis_index("leaf")
    row_index = lax.axis_index("row")
    col_index = lax.axis_index("col")
    local_front = front[0, :, 0, :, :, 0, :]
    row_slots = local_front.shape[0]
    col_slots = local_front.shape[2]
    pivot_tiles = NPIV // TILE
    assert pivot_tiles == row_count and pivot_tiles <= col_count
    row_tiles = jnp.arange(row_slots, dtype=jnp.int32) * row_count + row_index
    col_tiles = jnp.arange(col_slots, dtype=jnp.int32) * col_count + col_index
    working = local_front
    first_tiles = lax.all_gather(working[0, :, 0, :], "col", axis=0, tiled=False)
    diag_row = first_tiles[:pivot_tiles].transpose(1, 0, 2).reshape(TILE, NPIV)
    diagonal_block = lax.all_gather(diag_row, "row", axis=0, tiled=True)
    rest_cols, top_input, diagonal_block = lax.optimization_barrier(
        (working[1:, :, 0, :], working[0], diagonal_block)
    )
    first_cols = lax.all_gather(rest_cols, "col", axis=0, tiled=False)
    row_panel = first_cols[:pivot_tiles].transpose(1, 2, 0, 3).reshape(row_slots - 1, TILE, NPIV)
    top_rows = lax.all_gather(top_input, "row", axis=0, tiled=False)
    column_panel = top_rows.transpose(2, 3, 0, 1).reshape(col_slots, TILE, NPIV)
    stacked = jnp.concatenate([row_panel.reshape(-1, NPIV), column_panel.reshape(-1, NPIV)], axis=0)
    lower_factor, solved = tall_cholesky(diagonal_block, stacked)
    trailing_rows = (row_slots - 1) * TILE
    row_factor = solved[:trailing_rows].reshape(row_slots - 1, TILE, NPIV)
    column_factor = solved[trailing_rows:].reshape(col_slots, TILE, NPIV)
    column_factor = jnp.where((col_tiles >= pivot_tiles)[:, None, None], column_factor, 0.0)
    product = jnp.einsum(
        "atk,bsk->atbs",
        row_factor,
        column_factor,
        precision=HIGHEST,
        preferred_element_type=jnp.float32,
    )
    trailing = working[1:] - product
    own_col = jnp.minimum(col_index, pivot_tiles - 1)
    row_factor_cols = lax.dynamic_slice_in_dim(row_factor, own_col * TILE, TILE, 2)
    is_factor_col = (col_tiles < pivot_tiles)[None, None, :, None]
    trailing = jnp.where(is_factor_col, row_factor_cols[:, :, None, :], trailing)
    diag_rows = lax.dynamic_slice_in_dim(lower_factor, row_index * TILE, TILE, 0)
    diag_tile = lax.dynamic_slice_in_dim(diag_rows, own_col * TILE, TILE, 1)
    local_ids = jnp.arange(TILE, dtype=jnp.int32)
    global_row = row_index * TILE + local_ids[:, None]
    global_col = own_col * TILE + local_ids[None, :]
    diag_tile = jnp.where(global_row >= global_col, diag_tile, 0.0)
    top = jnp.where(is_factor_col[0], diag_tile[:, None, :], 0.0)
    top = jnp.broadcast_to(top, working[0].shape)
    working = jnp.concatenate([top[None], trailing], axis=0)
    factored = working.reshape(front.shape)
    contribution = jnp.where((col_tiles >= pivot_tiles)[None, None, :, None], working, 0.0)
    contrib_count = tile_map.shape[1]
    entry_ids = jnp.arange(contrib_count, dtype=jnp.int32)
    own_map = lax.dynamic_index_in_dim(tile_map, leaf_index, 0, keepdims=False)
    row_match = (row_tiles - pivot_tiles)[:, None] == entry_ids[None, :]
    row_targets = jnp.sum(jnp.where(row_match, own_map[None, :], 0), axis=1)
    row_valid = row_tiles >= pivot_tiles
    owner_count = leaf_count * row_count
    destination = row_targets % owner_count
    parent_row_slot = row_targets // owner_count
    slot_ids = jnp.arange(row_slots, dtype=jnp.int32)
    same_before = (
        (destination[None, :] == destination[:, None])
        & row_valid[None, :]
        & (slot_ids[None, :] < slot_ids[:, None])
    )
    rank_in_dest = jnp.sum(same_before.astype(jnp.int32), axis=1)
    capacity = (col_slots + row_count - 1) // row_count
    owner_ids = jnp.arange(owner_count, dtype=jnp.int32)
    capacity_ids = jnp.arange(capacity, dtype=jnp.int32)
    selection = (
        row_valid[None, None, :]
        & (destination[None, None, :] == owner_ids[:, None, None])
        & (rank_in_dest[None, None, :] == capacity_ids[None, :, None])
    )
    flattened = contribution.reshape(row_slots, -1)
    send_buffer = jnp.einsum(
        "oka,ax->okx",
        selection.astype(jnp.float32),
        flattened,
        precision=HIGHEST,
        preferred_element_type=jnp.float32,
    )
    chosen_slot = jnp.sum(jnp.where(selection, parent_row_slot[None, None, :], 0), axis=2)
    send_slots = jnp.where(jnp.any(selection, axis=2), chosen_slot, -1)
    received, received_slots = (
        lax.all_to_all(send_buffer, ("leaf", "row"), split_axis=0, concat_axis=0, tiled=True),
        lax.all_to_all(send_slots, ("leaf", "row"), split_axis=0, concat_axis=0, tiled=True),
    )
    received = received.reshape(leaf_count, row_count, capacity, -1)
    received_slots = received_slots.reshape(leaf_count, row_count, capacity)
    parent_local = parent[:, 0, 0, :, :, 0, :]
    parent_rows = parent_local.shape[0]
    parent_cols = parent_local.shape[2]
    row_place = (
        received_slots[None] == jnp.arange(parent_rows, dtype=jnp.int32)[:, None, None, None]
    ).astype(jnp.float32)
    by_leaf = jnp.einsum(
        "slrk,lrkx->slx", row_place, received, precision=HIGHEST, preferred_element_type=jnp.float32
    )
    by_leaf = by_leaf.reshape(parent_rows, leaf_count, TILE, col_slots, TILE)
    col_match = (col_tiles - pivot_tiles)[:, None] == entry_ids[None, :]
    col_targets = jnp.sum(jnp.where(col_match[None], tile_map[:, None, :], 0), axis=2)
    col_valid = col_tiles >= pivot_tiles
    parent_slot_ids = jnp.arange(parent_cols, dtype=jnp.int32)
    col_place = (
        col_valid[None, None, :]
        & (col_targets[:, None, :] // col_count == parent_slot_ids[None, :, None])
    ).astype(jnp.float32)
    assembled = jnp.einsum(
        "sltbv,lub->stuv", by_leaf, col_place, precision=HIGHEST, preferred_element_type=jnp.float32
    )
    new_parent = (parent_local + assembled).reshape(parent.shape)
    return (factored, new_parent)


def solution(mesh):
    return jax.shard_map(
        per_device,
        mesh=mesh,
        in_specs=(
            P("leaf", None, "row", None, None, "col", None),
            P(None, "leaf", "row", None, None, "col", None),
            P(),
            P(),
        ),
        out_specs=(
            P("leaf", None, "row", None, None, "col", None),
            P(None, "leaf", "row", None, None, "col", None),
        ),
        check_vma=False,
    )
```

profile of v0, /device:TPU:1, one launch (start us, length us, event | category | flops | bytes accessed | tf_op | source)
XLA Modules:
  0.0 557.9 jit_solution(11037079520208860323)
XLA Ops:
  7.2 1.9 copy.164
  9.9 51.3 %all-gather.10.cloned.1.call-done = f32[16,128,1,128]{3,1,2,0:T(8,128)} async-done(((f32[1,128,1,128]{3,1,2,0:T(8,128)}), f32[16,128,1,128]{3,1,2,0:T(8,128)}) %all-gather.10.cloned.1.call-update) | async-done | bytes 1048592 | tf_op jit(solution)/shard_map/all_gather | solution.py:91
  65.8 58.1 %all-gather.8.cloned.1.call-done = f32[1024,1024]{0,1:T(8,128)} async-done(((f32[128,1024]{0,1:T(8,128)}), f32[1024,1024]{0,1:T(8,128)}) %all-gather.8.cloned.1.call-update) | async-done | bytes 4194320 | tf_op jit(solution)/shard_map/all_gather | solution.py:93
  125.8 8.8 %all-to-all-start.1 = ((s32[16,1,1]{2,1,0:T(1,128)}), s32[16,1,1]{2,1,0:T(1,128)S(1)}, u32[]{:S(2)}, u32[]{:S(2)}) async-start(s32[16,1,1]{2,1,0:T(1,128)} %copy.138), calls=%async_computation.1 | async-start | bytes 16384 | tf_op jit(solution)/shard_map/all_to_all | solution.py:166
  139.9 11.7 %cholesky.134 = f32[128,128]{1,0:T(8,128)S(1)} custom-call(f32[128,128]{1,0:T(8,128)S(1)} %fusion.68), custom_call_target="Cholesky" | custom-call | tf_op jit(solution)/shard_map/jit(cholesky)/cholesky | solution.py:39
  153.6 9.8 %custom-call.12 = f32[1,128,128]{1,2,0:T(8,128)S(1)} custom-call(f32[1,128,128]{2,1,0:T(8,128)S(1)} %get-tuple-element.34), custom_call_target="InvertDiagBlocksLowerTriangular" | custom-call | tf_op jit(solution)/shard_map/triangular_solve/custom-call.0 | solution.py:40
  164.3 1.9 fusion.23
  167.0 4.6 slice_subtract_fusion.2
  171.7 12.0 %cholesky.145 = f32[128,128]{1,0:T(8,128)S(1)} custom-call(f32[128,128]{1,0:T(8,128)S(1)} %fusion.66), custom_call_target="Cholesky" | custom-call | tf_op jit(solution)/shard_map/jit(cholesky)/cholesky | solution.py:39
  185.7 9.8 %custom-call.13 = f32[1,128,128]{1,2,0:T(8,128)S(1)} custom-call(f32[1,128,128]{2,1,0:T(8,128)S(1)} %get-tuple-element.32), custom_call_target="InvertDiagBlocksLowerTriangular" | custom-call | tf_op jit(solution)/shard_map/triangular_solve/custom-call.0 | solution.py:40
  197.3 2.0 slice_subtract_fusion.3
  201.7 11.7 %cholesky.156 = f32[128,128]{1,0:T(8,128)S(1)} custom-call(f32[128,128]{1,0:T(8,128)S(1)} %fusion.64), custom_call_target="Cholesky" | custom-call | tf_op jit(solution)/shard_map/jit(cholesky)/cholesky | solution.py:39
  215.4 10.0 %custom-call.14 = f32[1,128,128]{1,2,0:T(8,128)S(1)} custom-call(f32[1,128,128]{2,1,0:T(8,128)S(1)} %get-tuple-element.30), custom_call_target="InvertDiagBlocksLowerTriangular" | custom-call | tf_op jit(solution)/shard_map/triangular_solve/custom-call.0 | solution.py:40
  228.0 2.9 slice_subtract_fusion.4
  231.0 11.7 %cholesky.167 = f32[128,128]{1,0:T(8,128)S(1)} custom-call(f32[128,128]{1,0:T(8,128)S(1)} %fusion.62), custom_call_target="Cholesky" | custom-call | tf_op jit(solution)/shard_map/jit(cholesky)/cholesky | solution.py:39
  244.7 9.8 %custom-call.15 = f32[1,128,128]{1,2,0:T(8,128)S(1)} custom-call(f32[1,128,128]{2,1,0:T(8,128)S(1)} %get-tuple-element.28), custom_call_target="InvertDiagBlocksLowerTriangular" | custom-call | tf_op jit(solution)/shard_map/triangular_solve/custom-call.0 | solution.py:40
  257.2 11.9 %cholesky.178 = f32[128,128]{1,0:T(8,128)S(1)} custom-call(f32[128,128]{1,0:T(8,128)S(1)} %fusion.60), custom_call_target="Cholesky" | custom-call | tf_op jit(solution)/shard_map/jit(cholesky)/cholesky | solution.py:39
  271.1 9.8 %custom-call.16 = f32[1,128,128]{1,2,0:T(8,128)S(1)} custom-call(f32[1,128,128]{2,1,0:T(8,128)S(1)} %get-tuple-element.26), custom_call_target="InvertDiagBlocksLowerTriangular" | custom-call | tf_op jit(solution)/shard_map/triangular_solve/custom-call.0 | solution.py:40
  282.5 11.7 %cholesky.189 = f32[128,128]{1,0:T(8,128)S(1)} custom-call(f32[128,128]{1,0:T(8,128)S(1)} %fusion.58), custom_call_target="Cholesky" | custom-call | tf_op jit(solution)/shard_map/jit(cholesky)/cholesky | solution.py:39
  295.6 9.8 %custom-call.17 = f32[1,128,128]{1,2,0:T(8,128)S(1)} custom-call(f32[1,128,128]{2,1,0:T(8,128)S(1)} %get-tuple-element.24), custom_call_target="InvertDiagBlocksLowerTriangular" | custom-call | tf_op jit(solution)/shard_map/triangular_solve/custom-call.0 | solution.py:40
  309.0 11.7 %cholesky.200 = f32[128,128]{1,0:T(8,128)S(1)} custom-call(f32[128,128]{1,0:T(8,128)S(1)} %fusion.56), custom_call_target="Cholesky" | custom-call | tf_op jit(solution)/shard_map/jit(cholesky)/cholesky | solution.py:39
  322.1 9.8 %custom-call.18 = f32[1,128,128]{1,2,0:T(8,128)S(1)} custom-call(f32[1,128,128]{2,1,0:T(8,128)S(1)} %get-tuple-element.22), custom_call_target="InvertDiagBlocksLowerTriangular" | custom-call | tf_op jit(solution)/shard_map/triangular_solve/custom-call.0 | solution.py:40
  332.9 11.7 %cholesky.211 = f32[128,128]{1,0:T(8,128)S(1)} custom-call(f32[128,128]{1,0:T(8,128)S(1)} %fusion.54), custom_call_target="Cholesky" | custom-call | tf_op jit(solution)/shard_map/jit(cholesky)/cholesky | solution.py:39
  345.9 10.0 %custom-call.19 = f32[1,128,128]{1,2,0:T(8,128)S(1)} custom-call(f32[1,128,128]{2,1,0:T(8,128)S(1)} %get-tuple-element.20), custom_call_target="InvertDiagBlocksLowerTriangular" | custom-call | tf_op jit(solution)/shard_map/triangular_solve/custom-call.0 | solution.py:40
  360.8 2.3 copy.132
  363.2 2.0 slice-done
  365.2 2.1 copy.131
  369.8 5.4 slice_subtract_fusion
  376.1 3.8 slice_subtract_fusion.1
  380.7 3.9 convolution_subtract_fusion
  385.5 3.0 convolution_subtract_fusion.1
  389.4 2.5 convolution_subtract_fusion.2
  397.1 2.5 copy-done.6
  399.6 2.1 slice.222
  401.8 5.1 copy.133
  407.9 1.8 slice_select_fusion
  409.7 1.8 copy.152
  411.6 8.9 %fusion.5 = f32[7,128,4,128]{3,1,2,0:T(8,128)S(1)} fusion(f32[1,8,1,128,4,1,128]{6,3,4,1,5,2,0:T(8,128)} %copy-done.4, f32[7,128,1024,1]{2,1,3,0:T(8,128)} %bitcast.198, f32[4,128,1024,1]{2,1,0,3:T(8,128)} %bitcast.203, f32[7,128,128]{2,1,0:T(8,128)S(1)} %constant_dynamic-slice_fusion, pred[4]{0:T(512)(128)(4,1)S(1)} %copy-done.44), kind=kOutput, calls=%fused_computation.23 | convolution fusion | flops 5638062080 | bytes 9895940 | tf_op jit(solution)/shard_map/atk,bsk->atbs/dot_general | solution.py:107
  420.6 2.4 copy.136
  423.0 3.7 concatenate.53
  426.8 3.8 convolution_bitcast_fusion
  430.6 6.3 %copy.137 = f32[16,1,65536]{2,1,0:T(1,128)} copy(f32[16,1,65536]{2,0,1:T(8,128)S(1)} %convolution_bitcast_fusion) | data formatting | bytes 8388608 | tf_op jit(solution)/shard_map/oka,ax->okx/dot_general | solution.py:155
  436.9 7.6 %all-to-all-start = ((f32[16,1,65536]{2,1,0:T(1,128)}), f32[16,1,65536]{2,1,0:T(1,128)}, u32[]{:S(2)}, u32[]{:S(2)}) async-start(f32[16,1,65536]{2,1,0:T(1,128)} %copy.137), calls=%async_computation | async-start | bytes 8388608 | tf_op jit(solution)/shard_map/all_to_all | solution.py:165
  445.6 3.5 copy.140
  449.1 88.1 %all-to-all-done = f32[16,1,65536]{2,1,0:T(1,128)} async-done(((f32[16,1,65536]{2,1,0:T(1,128)}), f32[16,1,65536]{2,1,0:T(1,128)}, u32[]{:S(2)}, u32[]{:S(2)}) %all-to-all-start) | async-done | bytes 4194336 | tf_op jit(solution)/shard_map/all_to_all | solution.py:165
  537.2 7.8 %convolution_bitcast_fusion.1 = f32[4,2,65536]{2,0,1:T(4,128)} fusion(f32[16,1,65536]{2,1,0:T(1,128)} %all-to-all-done, s32[2,8]{1,0:T(2,128)S(1)} %eq.153), kind=kOutput, calls=%fused_computation.1 | convolution fusion | flops 50331712 | bytes 6291520 | tf_op jit(solution)/shard_map/slrk,lrkx->slx/dot_general | solution.py:176
  545.0 3.1 reshape.454
  548.1 2.8 fusion.6
  (246 shorter events, 61.4 us)
Async XLA Ops:
  7.2 116.8 %copy-start.51 = (s32[2,56]{1,0:T(2,128)S(1)}, s32[2,56]{1,0:T(2,128)}, u32[]{:S(2)}) copy-start(s32[2,56]{1,0:T(2,128)} %param.9) | copy-start | bytes 1348
  7.2 54.0 %all-gather.10.cloned.1.call-start = ((), (), s32[]{:S(2)}) async-start(), calls=%async_computation.3 | async-start | bytes 1114112 | tf_op jit(solution)/shard_map/all_gather | solution.py:91
  9.1 154.6 %copy-start.4 = (f32[1,8,1,128,4,1,128]{6,3,4,1,5,2,0:T(8,128)}, f32[1,8,1,128,4,1,128]{6,3,4,1,5,2,0:T(8,128)S(1)}, u32[]{:S(2)}) copy-start(f32[1,8,1,128,4,1,128]{6,3,4,1,5,2,0:T(8,128)S(1)} %copy.164) | copy-start | bytes 6291460
  9.8 114.1 %all-gather.8.cloned.1.call-start = ((), (), s32[]{:S(2)}) async-start(), calls=%async_computation.2 | async-start | bytes 4718592 | tf_op jit(solution)/shard_map/all_gather | solution.py:93
  63.2 297.6 %all-gather.14.cloned.1.call-start = ((), (), s32[]{:S(2)}) async-start(), calls=%async_computation.5 | async-start | bytes 2359296 | tf_op jit(solution)/shard_map/all_gather | solution.py:99
  123.9 239.2 %all-gather.12.cloned.1.call-start = ((), (), s32[]{:S(2)}) async-start(), calls=%async_computation.4 | async-start | bytes 7798784 | tf_op jit(solution)/shard_map/all_gather | solution.py:97
  125.8 311.2 %all-to-all-start.1 = ((s32[16,1,1]{2,1,0:T(1,128)}), s32[16,1,1]{2,1,0:T(1,128)S(1)}, u32[]{:S(2)}, u32[]{:S(2)}) async-start(s32[16,1,1]{2,1,0:T(1,128)} %copy.138), calls=%async_computation.1 | async-start | bytes 16384 | tf_op jit(solution)/shard_map/all_to_all | solution.py:166
  197.3 2.1 copy-start.2
  257.0 98.9 %copy-start.1 = (f32[896,128]{1,0:T(8,128)S(1)}, f32[896,128]{1,0:T(8,128)}, u32[]{:S(2)}) copy-start(f32[896,128]{1,0:T(8,128)} %copy-done) | copy-start | bytes 1376260
  269.8 87.1 %copy-start.3 = (f32[768,128]{1,0:T(8,128)S(1)}, f32[768,128]{1,0:T(8,128)}, u32[]{:S(2)}) copy-start(f32[768,128]{1,0:T(8,128)} %copy-done.2) | copy-start | bytes 1179652
  281.2 76.5 %copy-start.18 = (f32[128,128]{1,0:T(8,128)}, f32[128,128]{1,0:T(8,128)S(1)}, u32[]{:S(2)}) copy-start(f32[128,128]{1,0:T(8,128)S(1)} %fusion.37) | copy-start | bytes 196612
  281.7 76.5 %copy-start.7 = (f32[384,128]{1,0:T(8,128)}, f32[384,128]{1,0:T(8,128)S(1)}, u32[]{:S(2)}) copy-start(f32[384,128]{1,0:T(8,128)S(1)} %fusion.47) | copy-start | bytes 589828
  282.4 23.1 %copy-start.11 = (f32[384,384]{0,1:T(8,128)}, f32[384,384]{0,1:T(8,128)S(1)}, u32[]{:S(2)}) copy-start(f32[384,384]{0,1:T(8,128)S(1)} %convolution_subtract_fusion.6) | copy-start | bytes 1769476
  282.4 75.4 %copy-start.32 = (f32[128,128]{1,0:T(8,128)S(1)}, f32[128,128]{1,0:T(8,128)}, u32[]{:S(2)}) copy-start(f32[128,128]{1,0:T(8,128)} %get-tuple-element.31) | copy-start | bytes 196612
  282.4 75.4 %copy-start.36 = (f32[1024]{0:T(1024)S(1)}, f32[1024]{0:T(1024)}, u32[]{:S(2)}) copy-start(f32[1024]{0:T(1024)} %pad.10.clone) | copy-start | bytes 12292
  282.4 75.6 %copy-start.35 = (f32[128,128]{1,0:T(8,128)S(1)}, f32[128,128]{1,0:T(8,128)}, u32[]{:S(2)}) copy-start(f32[128,128]{1,0:T(8,128)} %get-tuple-element.29) | copy-start | bytes 196612
  282.4 75.6 %copy-start.38 = (f32[1024]{0:T(1024)S(1)}, f32[1024]{0:T(1024)}, u32[]{:S(2)}) copy-start(f32[1024]{0:T(1024)} %pad.13.clone) | copy-start | bytes 12292
  294.3 63.9 %copy-start.33 = (f32[128,128]{1,0:T(8,128)S(1)}, f32[128,128]{1,0:T(8,128)}, u32[]{:S(2)}) copy-start(f32[128,128]{1,0:T(8,128)} %get-tuple-element.27) | copy-start | bytes 196612
  294.3 63.9 %copy-start.37 = (f32[1024]{0:T(1024)S(1)}, f32[1024]{0:T(1024)}, u32[]{:S(2)}) copy-start(f32[1024]{0:T(1024)} %pad.16.clone) | copy-start | bytes 12292
  306.1 52.3 %copy-start.20 = (f32[128,128]{1,0:T(8,128)}, f32[128,128]{1,0:T(8,128)S(1)}, u32[]{:S(2)}) copy-start(f32[128,128]{1,0:T(8,128)S(1)} %fusion.35) | copy-start | bytes 196612
  307.5 51.0 %copy-start.9 = (f32[256,128]{1,0:T(8,128)}, f32[256,128]{1,0:T(8,128)S(1)}, u32[]{:S(2)}) copy-start(f32[256,128]{1,0:T(8,128)S(1)} %fusion.49) | copy-start | bytes 393220
  332.2 26.8 %copy-start.24 = (f32[128,128]{1,0:T(8,128)}, f32[128,128]{1,0:T(8,128)S(1)}, u32[]{:S(2)}) copy-start(f32[128,128]{1,0:T(8,128)S(1)} %fusion.33) | copy-start | bytes 196612
  332.5 26.5 %copy-start.12 = (f32[128,128]{1,0:T(8,128)}, f32[128,128]{1,0:T(8,128)S(1)}, u32[]{:S(2)}) copy-start(f32[128,128]{1,0:T(8,128)S(1)} %fusion.51) | copy-start | bytes 196612
  332.7 26.2 %copy-start.49 = (s32[128]{0:T(128)S(1)}, s32[128]{0:T(128)}, u32[]{:S(2)}) copy-start(s32[128]{0:T(128)} %get-tuple-element.56) | copy-start | bytes 1540
  332.8 26.2 %copy-start.50 = (s32[128]{0:T(128)S(1)}, s32[128]{0:T(128)}, u32[]{:S(2)}) copy-start(s32[128]{0:T(128)} %get-tuple-element.57) | copy-start | bytes 1540
  332.9 27.1 %copy-start.43 = (pred[4]{0:T(512)(128)(4,1)S(1)}, pred[4]{0:T(512)(128)(4,1)}, u32[]{:S(2)}) copy-start(pred[4]{0:T(512)(128)(4,1)} %get-tuple-element.55) | copy-start | bytes 16
  369.8 5.4 copy-start.27
  376.1 3.8 copy-start.29
  380.7 4.0 copy-start.17
  385.5 3.0 copy-start.19
  385.5 3.9 copy-start.8
  388.5 3.4 copy-start.21
  389.4 3.4 copy-start.10
  391.9 2.2 copy-start.25
  391.9 3.0 copy-start.13
  392.8 3.5 copy-start.34
  397.1 2.5 copy-start.6
  401.8 6.1 %copy-start.53 = (pred[512]{0:T(512)(128)(4,1)S(1)}, pred[512]{0:T(512)(128)(4,1)}, u32[]{:S(2)}) copy-start(pred[512]{0:T(512)(128)(4,1)} %broadcast_bitcast_fusion) | copy-start | bytes 1540
  407.9 3.7 copy-start.44
  420.5 6.2 %copy-start.48 = (pred[4]{0:T(512)(128)(4,1)S(1)}, pred[4]{0:T(512)(128)(4,1)}, u32[]{:S(2)}) copy-start(pred[4]{0:T(512)(128)(4,1)} %copy-done.47) | copy-start | bytes 16
  420.5 6.3 %copy-start.15 = (f32[128,4,128]{2,1,0:T(4,128)S(1)}, f32[128,4,128]{2,1,0:T(4,128)}, u32[]{:S(2)}) copy-start(f32[128,4,128]{2,1,0:T(4,128)} %broadcast_select_fusion) | copy-start | bytes 786436
  420.5 6.3 %copy-start.40 = (s32[8]{0:T(128)S(1)}, s32[8]{0:T(128)}, u32[]{:S(2)}) copy-start(s32[8]{0:T(128)} %copy-done.39) | copy-start | bytes 100
  420.5 6.3 %copy-start.42 = (pred[8]{0:T(512)(128)(4,1)S(1)}, pred[8]{0:T(512)(128)(4,1)}, u32[]{:S(2)}) copy-start(pred[8]{0:T(512)(128)(4,1)} %copy-done.41) | copy-start | bytes 28
  420.6 6.3 %copy-start.46 = (pred[8]{0:T(512)(128)(4,1)S(1)}, pred[8]{0:T(512)(128)(4,1)}, u32[]{:S(2)}) copy-start(pred[8]{0:T(512)(128)(4,1)} %copy-done.45) | copy-start | bytes 28
  436.9 7.7 %copy-start.52 = (s32[2,56]{1,0:T(2,128)S(1)}, s32[2,56]{1,0:T(2,128)}, u32[]{:S(2)}) copy-start(s32[2,56]{1,0:T(2,128)} %param.9) | copy-start | bytes 1348
  436.9 8.4 %copy-start.23 = (f32[128,128]{1,0:T(8,128)S(1)}, f32[128,128]{1,0:T(8,128)}, u32[]{:S(2)}) copy-start(f32[128,128]{1,0:T(8,128)} %copy-done.22) | copy-start | bytes 196612
  436.9 100.2 %all-to-all-start = ((f32[16,1,65536]{2,1,0:T(1,128)}), f32[16,1,65536]{2,1,0:T(1,128)}, u32[]{:S(2)}, u32[]{:S(2)}) async-start(f32[16,1,65536]{2,1,0:T(1,128)} %copy.137), calls=%async_computation | async-start | bytes 8388608 | tf_op jit(solution)/shard_map/all_to_all | solution.py:165
  545.0 3.1 copy-start.14
  (13 other events, 11.6 us)
Sparse Core Ops, SparseCore 0:
  11.0 50.0 all-gather.9
  63.4 60.4 all-gather.7
  125.7 38.9 all-gather.13
  167.0 73.5 all-gather.11
where the time goes:
time: 568 us; the launch traced here: 558 us
  waiting for transfers between devices  198 us (35%)
  other arithmetic  197 us (35%)
  matrix products  74.3 us (13%)
  local copies, waits for them, and re-layouts  57.1 us (10%)
  starting transfers between devices  16.6 us (3%)
  between operations  15.6 us (3%)
    another operation x24, other arithmetic, tall_cholesky(): pivot_factor = jnp.linalg.cholesky(pivot)  99.6 us
    all_to_all x1, waiting for transfers between devices, per_device(): lax.all_to_all(send_buffer, ('leaf', 'row'), split_axis=0, concat_axis=0,...  88.1 us
    another operation x16, other arithmetic, tall_cholesky(): lax.linalg.triangular_solve(pivot_factor, eye, left_side=True, lower=True)  87.2 us
    all_gather x1, waiting for transfers between devices, per_device(): diagonal_block = lax.all_gather(diag_row, 'row', axis=0, tiled=True)  58.1 us
    all_gather x1, waiting for transfers between devices, per_device(): lax.all_gather(working[0, :, 0, :], 'col', axis=0, tiled=False)  51.3 us
    dot_general x7, matrix products, tall_cholesky(): jnp.dot(solved, lower_factor[low + TILE:, low:low + TILE].T, precision=HI...  21.2 us
    unnamed x111, local copies, waits for them, and re-layouts  14.3 us
    dot_general x7, matrix products, tall_cholesky(): jnp.dot(solved, solved.T, precision=HIGHEST, preferred_element_type=jnp.f...  12.8 us
  transfers between devices with their start and end apart: 6, of which 3 were waited for; matrix products, arithmetic and copies ran while one was open for 54% of the time, Pallas kernels for 0%

commit v1 on v0

--- a/solution.py
+++ b/solution.py
@@ -90,7 +90,9 @@
     working = local_front
     first_tiles = lax.all_gather(working[0, :, 0, :], "col", axis=0, tiled=False)
     diag_row = first_tiles[:pivot_tiles].transpose(1, 0, 2).reshape(TILE, NPIV)
-    diagonal_block = lax.all_gather(diag_row, "row", axis=0, tiled=True)
+    diagonal_block = jnp.concatenate(
+        lax.all_to_all(jnp.stack([diag_row] * lax.axis_size("row")), "row", 0, 0), axis=0
+    )
     rest_cols, top_input, diagonal_block = lax.optimization_barrier(
         (working[1:, :, 0, :], working[0], diagonal_block)
     )

time: 568 us -> 613 us (1.079)
  waiting for transfers between devices: 198 us -> 234 us
  local copies, waits for them, and re-layouts: 57.1 us -> 63.4 us
    all_to_all x0 -> x1, waiting for transfers between devices: none -> 94.3 us  [per_device(): lax.all_to_all(jnp.stack([diag_row] * lax.axis_size('row')), 'row', 0, 0)]
    all_gather x1 -> x0, waiting for transfers between devices: 58.1 us -> none  [per_device(): diagonal_block = lax.all_gather(diag_row, 'row', axis=0, tiled=True)]
    all_to_all x0 -> x1, starting transfers between devices: none -> 6.73 us  [per_device(): lax.all_to_all(jnp.stack([diag_row] * lax.axis_size('row')), 'row', 0, 0)]
    unnamed x111 -> x112, local copies, waits for them, and re-layouts: 14.3 us -> 14.6 us
  transfers between devices with their start and end apart: 6 -> 6, of which waited for: 3 -> 3; matrix products, arithmetic and copies ran while one was open for 54% -> 50% of each run, Pallas kernels for 0% -> 0%
where the time goes in v1:
time: 613 us; the launch traced here: 602 us
  waiting for transfers between devices  234 us (38%)
  other arithmetic  197 us (32%)
  matrix products  74.3 us (12%)
  local copies, waits for them, and re-layouts  63.4 us (10%)
  starting transfers between devices  18.2 us (3%)
  between operations  15.6 us (3%)
    another operation x24, other arithmetic, tall_cholesky(): pivot_factor = jnp.linalg.cholesky(pivot)  99.6 us
    all_to_all x1, waiting for transfers between devices, per_device(): lax.all_to_all(jnp.stack([diag_row] * lax.axis_size('row')), 'row', 0, 0)  94.3 us
    all_to_all x1, waiting for transfers between devices, per_device(): lax.all_to_all(send_buffer, ('leaf', 'row'), split_axis=0, concat_axis=0,...  88.1 us
    another operation x16, other arithmetic, tall_cholesky(): lax.linalg.triangular_solve(pivot_factor, eye, left_side=True, lower=True)  87 us
    all_gather x1, waiting for transfers between devices, per_device(): lax.all_gather(working[0, :, 0, :], 'col', axis=0, tiled=False)  51.3 us
    dot_general x7, matrix products, tall_cholesky(): jnp.dot(solved, lower_factor[low + TILE:, low:low + TILE].T, precision=HI...  21.2 us
    unnamed x112, local copies, waits for them, and re-layouts  14.6 us
    dot_general x7, matrix products, tall_cholesky(): jnp.dot(solved, solved.T, precision=HIGHEST, preferred_element_type=jnp.f...  12.8 us
  transfers between devices with their start and end apart: 6, of which 3 were waited for; matrix products, arithmetic and copies ran while one was open for 50% of the time, Pallas kernels for 0%

profile of v1, /device:TPU:1, one launch (start us, length us, event | category | flops | bytes accessed | tf_op | source)
XLA Modules:
  0.0 601.8 jit_solution(5237408563387931805)
XLA Ops:
  9.8 51.3 %all-gather.7.cloned.1.call-done = f32[16,128,1,128]{3,1,2,0:T(8,128)} async-done(((f32[1,128,1,128]{3,1,2,0:T(8,128)}), f32[16,128,1,128]{3,1,2,0:T(8,128)}) %all-gather.7.cloned.1.call-update) | async-done | bytes 1048592 | tf_op jit(solution)/shard_map/all_gather | solution.py:91
  62.4 2.3 stack.3
  64.7 6.7 %all-to-all-start = ((f32[8,128,1024]{1,2,0:T(8,128)}), f32[8,128,1024]{1,2,0:T(8,128)}, u32[]{:S(2)}, u32[]{:S(2)}) async-start(f32[8,128,1024]{1,2,0:T(8,128)} %stack.3), calls=%async_computation | async-start | bytes 8388608 | tf_op jit(solution)/shard_map/all_to_all | solution.py:94
  74.0 94.3 %all-to-all-done = f32[8,128,1024]{1,2,0:T(8,128)} async-done(((f32[8,128,1024]{1,2,0:T(8,128)}), f32[8,128,1024]{1,2,0:T(8,128)}, u32[]{:S(2)}, u32[]{:S(2)}) %all-to-all-start) | async-done | bytes 4194336 | tf_op jit(solution)/shard_map/all_to_all | solution.py:94
  168.3 4.8 copy_bitcast_fusion
  175.0 3.7 all-to-all-start.2
  184.1 11.7 %cholesky.134 = f32[128,128]{1,0:T(8,128)S(1)} custom-call(f32[128,128]{1,0:T(8,128)S(1)} %fusion.68), custom_call_target="Cholesky" | custom-call | tf_op jit(solution)/shard_map/jit(cholesky)/cholesky | solution.py:39
  197.7 9.8 %custom-call.12 = f32[1,128,128]{1,2,0:T(8,128)S(1)} custom-call(f32[1,128,128]{2,1,0:T(8,128)S(1)} %get-tuple-element.34), custom_call_target="InvertDiagBlocksLowerTriangular" | custom-call | tf_op jit(solution)/shard_map/triangular_solve/custom-call.0 | solution.py:40
  208.5 1.9 fusion.23
  211.1 4.6 slice_subtract_fusion.2
  215.9 12.0 %cholesky.145 = f32[128,128]{1,0:T(8,128)S(1)} custom-call(f32[128,128]{1,0:T(8,128)S(1)} %fusion.66), custom_call_target="Cholesky" | custom-call | tf_op jit(solution)/shard_map/jit(cholesky)/cholesky | solution.py:39
  229.9 9.8 %custom-call.13 = f32[1,128,128]{1,2,0:T(8,128)S(1)} custom-call(f32[1,128,128]{2,1,0:T(8,128)S(1)} %get-tuple-element.32), custom_call_target="InvertDiagBlocksLowerTriangular" | custom-call | tf_op jit(solution)/shard_map/triangular_solve/custom-call.0 | solution.py:40
  241.4 2.0 slice_subtract_fusion.3
  245.9 11.7 %cholesky.156 = f32[128,128]{1,0:T(8,128)S(1)} custom-call(f32[128,128]{1,0:T(8,128)S(1)} %fusion.64), custom_call_target="Cholesky" | custom-call | tf_op jit(solution)/shard_map/jit(cholesky)/cholesky | solution.py:39
  259.5 10.0 %custom-call.14 = f32[1,128,128]{1,2,0:T(8,128)S(1)} custom-call(f32[1,128,128]{2,1,0:T(8,128)S(1)} %get-tuple-element.30), custom_call_target="InvertDiagBlocksLowerTriangular" | custom-call | tf_op jit(solution)/shard_map/triangular_solve/custom-call.0 | solution.py:40
  272.1 3.0 slice_subtract_fusion.4
  275.2 11.7 %cholesky.167 = f32[128,128]{1,0:T(8,128)S(1)} custom-call(f32[128,128]{1,0:T(8,128)S(1)} %fusion.62), custom_call_target="Cholesky" | custom-call | tf_op jit(solution)/shard_map/jit(cholesky)/cholesky | solution.py:39
  288.9 9.8 %custom-call.15 = f32[1,128,128]{1,2,0:T(8,128)S(1)} custom-call(f32[1,128,128]{2,1,0:T(8,128)S(1)} %get-tuple-element.28), custom_call_target="InvertDiagBlocksLowerTriangular" | custom-call | tf_op jit(solution)/shard_map/triangular_solve/custom-call.0 | solution.py:40
  301.3 11.9 %cholesky.178 = f32[128,128]{1,0:T(8,128)S(1)} custom-call(f32[128,128]{1,0:T(8,128)S(1)} %fusion.60), custom_call_target="Cholesky" | custom-call | tf_op jit(solution)/shard_map/jit(cholesky)/cholesky | solution.py:39
  315.2 9.8 %custom-call.16 = f32[1,128,128]{1,2,0:T(8,128)S(1)} custom-call(f32[1,128,128]{2,1,0:T(8,128)S(1)} %get-tuple-element.26), custom_call_target="InvertDiagBlocksLowerTriangular" | custom-call | tf_op jit(solution)/shard_map/triangular_solve/custom-call.0 | solution.py:40
  326.7 11.7 %cholesky.189 = f32[128,128]{1,0:T(8,128)S(1)} custom-call(f32[128,128]{1,0:T(8,128)S(1)} %fusion.58), custom_call_target="Cholesky" | custom-call | tf_op jit(solution)/shard_map/jit(cholesky)/cholesky | solution.py:39
  339.6 9.8 %custom-call.17 = f32[1,128,128]{1,2,0:T(8,128)S(1)} custom-call(f32[1,128,128]{2,1,0:T(8,128)S(1)} %get-tuple-element.24), custom_call_target="InvertDiagBlocksLowerTriangular" | custom-call | tf_op jit(solution)/shard_map/triangular_solve/custom-call.0 | solution.py:40
  353.0 11.7 %cholesky.200 = f32[128,128]{1,0:T(8,128)S(1)} custom-call(f32[128,128]{1,0:T(8,128)S(1)} %fusion.56), custom_call_target="Cholesky" | custom-call | tf_op jit(solution)/shard_map/jit(cholesky)/cholesky | solution.py:39
  366.0 9.8 %custom-call.18 = f32[1,128,128]{1,2,0:T(8,128)S(1)} custom-call(f32[1,128,128]{2,1,0:T(8,128)S(1)} %get-tuple-element.22), custom_call_target="InvertDiagBlocksLowerTriangular" | custom-call | tf_op jit(solution)/shard_map/triangular_solve/custom-call.0 | solution.py:40
  376.9 11.7 %cholesky.211 = f32[128,128]{1,0:T(8,128)S(1)} custom-call(f32[128,128]{1,0:T(8,128)S(1)} %fusion.54), custom_call_target="Cholesky" | custom-call | tf_op jit(solution)/shard_map/jit(cholesky)/cholesky | solution.py:39
  389.9 9.9 %custom-call.19 = f32[1,128,128]{1,2,0:T(8,128)S(1)} custom-call(f32[1,128,128]{2,1,0:T(8,128)S(1)} %get-tuple-element.20), custom_call_target="InvertDiagBlocksLowerTriangular" | custom-call | tf_op jit(solution)/shard_map/triangular_solve/custom-call.0 | solution.py:40
  404.8 2.3 copy.134
  407.1 2.0 slice-done
  409.2 2.1 copy.133
  413.8 5.4 slice_subtract_fusion
  420.0 3.8 slice_subtract_fusion.1
  424.6 3.9 convolution_subtract_fusion
  429.4 3.0 convolution_subtract_fusion.1
  433.3 2.5 convolution_subtract_fusion.2
  441.1 2.5 copy-done.6
  443.6 2.2 slice.222
  445.7 5.0 copy.135
  455.5 8.9 %fusion.5 = f32[7,128,4,128]{3,1,2,0:T(8,128)S(1)} fusion(f32[1,8,1,128,4,1,128]{6,3,4,1,5,2,0:T(8,128)} %copy-done.4, f32[7,128,1024,1]{2,1,3,0:T(8,128)} %bitcast.203, f32[4,128,1024,1]{2,1,0,3:T(8,128)} %bitcast.208, f32[7,128,128]{2,1,0:T(8,128)S(1)} %constant_dynamic-slice_fusion, pred[4]{0:T(512)(128)(4,1)S(1)} %copy-done.44), kind=kOutput, calls=%fused_computation.24 | convolution fusion | flops 5638062080 | bytes 9895940 | tf_op jit(solution)/shard_map/atk,bsk->atbs/dot_general | solution.py:109
  464.5 2.5 copy.138
  466.9 3.7 concatenate.53
  470.8 3.8 convolution_bitcast_fusion
  474.5 6.3 %copy.139 = f32[16,1,65536]{2,1,0:T(1,128)} copy(f32[16,1,65536]{2,0,1:T(8,128)S(1)} %convolution_bitcast_fusion) | data formatting | bytes 8388608 | tf_op jit(solution)/shard_map/oka,ax->okx/dot_general | solution.py:157
  480.9 7.6 %all-to-all-start.1 = ((f32[16,1,65536]{2,1,0:T(1,128)}), f32[16,1,65536]{2,1,0:T(1,128)}, u32[]{:S(2)}, u32[]{:S(2)}) async-start(f32[16,1,65536]{2,1,0:T(1,128)} %copy.139), calls=%async_computation.1 | async-start | bytes 8388608 | tf_op jit(solution)/shard_map/all_to_all | solution.py:167
  489.5 3.5 copy.142
  493.0 88.1 %all-to-all-done.1 = f32[16,1,65536]{2,1,0:T(1,128)} async-done(((f32[16,1,65536]{2,1,0:T(1,128)}), f32[16,1,65536]{2,1,0:T(1,128)}, u32[]{:S(2)}, u32[]{:S(2)}) %all-to-all-start.1) | async-done | bytes 4194336 | tf_op jit(solution)/shard_map/all_to_all | solution.py:167
  581.1 7.8 %convolution_bitcast_fusion.1 = f32[4,2,65536]{2,0,1:T(4,128)} fusion(f32[16,1,65536]{2,1,0:T(1,128)} %all-to-all-done.1, s32[2,8]{1,0:T(2,128)S(1)} %eq.153), kind=kOutput, calls=%fused_computation.1 | convolution fusion | flops 50331712 | bytes 6291520 | tf_op jit(solution)/shard_map/slrk,lrkx->slx/dot_general | solution.py:178
  588.9 3.1 reshape.456
  592.1 2.8 fusion.6
  (247 shorter events, 65.9 us)
Async XLA Ops:
  7.2 54.0 %all-gather.7.cloned.1.call-start = ((), (), s32[]{:S(2)}) async-start(), calls=%async_computation.3 | async-start | bytes 1114112 | tf_op jit(solution)/shard_map/all_gather | solution.py:91
  9.1 64.1 %copy-start.4 = (f32[1,8,1,128,4,1,128]{6,3,4,1,5,2,0:T(8,128)}, f32[1,8,1,128,4,1,128]{6,3,4,1,5,2,0:T(8,128)S(1)}, u32[]{:S(2)}) copy-start(f32[1,8,1,128,4,1,128]{6,3,4,1,5,2,0:T(8,128)S(1)} %copy.169) | copy-start | bytes 6291460
  64.7 103.6 %all-to-all-start = ((f32[8,128,1024]{1,2,0:T(8,128)}), f32[8,128,1024]{1,2,0:T(8,128)}, u32[]{:S(2)}, u32[]{:S(2)}) async-start(f32[8,128,1024]{1,2,0:T(8,128)} %stack.3), calls=%async_computation | async-start | bytes 8388608 | tf_op jit(solution)/shard_map/all_to_all | solution.py:94
  71.4 333.4 %all-gather.11.cloned.1.call-start = ((), (), s32[]{:S(2)}) async-start(), calls=%async_computation.5 | async-start | bytes 2359296 | tf_op jit(solution)/shard_map/all_gather | solution.py:101
  74.0 99.2 %copy-start.51 = (s32[2,56]{1,0:T(2,128)S(1)}, s32[2,56]{1,0:T(2,128)}, u32[]{:S(2)}) copy-start(s32[2,56]{1,0:T(2,128)} %param.9) | copy-start | bytes 1348
  173.1 234.0 %all-gather.9.cloned.1.call-start = ((), (), s32[]{:S(2)}) async-start(), calls=%async_computation.4 | async-start | bytes 7798784 | tf_op jit(solution)/shard_map/all_gather | solution.py:99
  175.0 305.8 %all-to-all-start.2 = ((s32[16,1,1]{2,1,0:T(1,128)}), s32[16,1,1]{2,1,0:T(1,128)S(1)}, u32[]{:S(2)}, u32[]{:S(2)}) async-start(s32[16,1,1]{2,1,0:T(1,128)} %copy.140), calls=%async_computation.2 | async-start | bytes 16384 | tf_op jit(solution)/shard_map/all_to_all | solution.py:168
  241.4 2.1 copy-start.2
  301.2 98.7 %copy-start.1 = (f32[896,128]{1,0:T(8,128)S(1)}, f32[896,128]{1,0:T(8,128)}, u32[]{:S(2)}) copy-start(f32[896,128]{1,0:T(8,128)} %copy-done) | copy-start | bytes 1376260
  313.9 86.9 %copy-start.3 = (f32[768,128]{1,0:T(8,128)S(1)}, f32[768,128]{1,0:T(8,128)}, u32[]{:S(2)}) copy-start(f32[768,128]{1,0:T(8,128)} %copy-done.2) | copy-start | bytes 1179652
  325.3 76.4 %copy-start.18 = (f32[128,128]{1,0:T(8,128)}, f32[128,128]{1,0:T(8,128)S(1)}, u32[]{:S(2)}) copy-start(f32[128,128]{1,0:T(8,128)S(1)} %fusion.37) | copy-start | bytes 196612
  325.8 76.3 %copy-start.7 = (f32[384,128]{1,0:T(8,128)}, f32[384,128]{1,0:T(8,128)S(1)}, u32[]{:S(2)}) copy-start(f32[384,128]{1,0:T(8,128)S(1)} %fusion.47) | copy-start | bytes 589828
  326.5 22.9 %copy-start.11 = (f32[384,384]{0,1:T(8,128)}, f32[384,384]{0,1:T(8,128)S(1)}, u32[]{:S(2)}) copy-start(f32[384,384]{0,1:T(8,128)S(1)} %convolution_subtract_fusion.6) | copy-start | bytes 1769476
  326.5 75.2 %copy-start.32 = (f32[128,128]{1,0:T(8,128)S(1)}, f32[128,128]{1,0:T(8,128)}, u32[]{:S(2)}) copy-start(f32[128,128]{1,0:T(8,128)} %get-tuple-element.31) | copy-start | bytes 196612
  326.5 75.2 %copy-start.36 = (f32[1024]{0:T(1024)S(1)}, f32[1024]{0:T(1024)}, u32[]{:S(2)}) copy-start(f32[1024]{0:T(1024)} %pad.10.clone) | copy-start | bytes 12292
  326.5 75.4 %copy-start.35 = (f32[128,128]{1,0:T(8,128)S(1)}, f32[128,128]{1,0:T(8,128)}, u32[]{:S(2)}) copy-start(f32[128,128]{1,0:T(8,128)} %get-tuple-element.29) | copy-start | bytes 196612
  326.5 75.4 %copy-start.38 = (f32[1024]{0:T(1024)S(1)}, f32[1024]{0:T(1024)}, u32[]{:S(2)}) copy-start(f32[1024]{0:T(1024)} %pad.13.clone) | copy-start | bytes 12292
  338.4 63.8 %copy-start.33 = (f32[128,128]{1,0:T(8,128)S(1)}, f32[128,128]{1,0:T(8,128)}, u32[]{:S(2)}) copy-start(f32[128,128]{1,0:T(8,128)} %get-tuple-element.27) | copy-start | bytes 196612
  338.4 63.8 %copy-start.37 = (f32[1024]{0:T(1024)S(1)}, f32[1024]{0:T(1024)}, u32[]{:S(2)}) copy-start(f32[1024]{0:T(1024)} %pad.16.clone) | copy-start | bytes 12292
  350.1 52.3 %copy-start.20 = (f32[128,128]{1,0:T(8,128)}, f32[128,128]{1,0:T(8,128)S(1)}, u32[]{:S(2)}) copy-start(f32[128,128]{1,0:T(8,128)S(1)} %fusion.35) | copy-start | bytes 196612
  351.5 51.0 %copy-start.9 = (f32[256,128]{1,0:T(8,128)}, f32[256,128]{1,0:T(8,128)S(1)}, u32[]{:S(2)}) copy-start(f32[256,128]{1,0:T(8,128)S(1)} %fusion.49) | copy-start | bytes 393220
  376.1 26.8 %copy-start.24 = (f32[128,128]{1,0:T(8,128)}, f32[128,128]{1,0:T(8,128)S(1)}, u32[]{:S(2)}) copy-start(f32[128,128]{1,0:T(8,128)S(1)} %fusion.33) | copy-start | bytes 196612
  376.4 26.5 %copy-start.12 = (f32[128,128]{1,0:T(8,128)}, f32[128,128]{1,0:T(8,128)S(1)}, u32[]{:S(2)}) copy-start(f32[128,128]{1,0:T(8,128)S(1)} %fusion.51) | copy-start | bytes 196612
  376.7 26.2 %copy-start.49 = (s32[128]{0:T(128)S(1)}, s32[128]{0:T(128)}, u32[]{:S(2)}) copy-start(s32[128]{0:T(128)} %get-tuple-element.56) | copy-start | bytes 1540
  376.7 26.2 %copy-start.50 = (s32[128]{0:T(128)S(1)}, s32[128]{0:T(128)}, u32[]{:S(2)}) copy-start(s32[128]{0:T(128)} %get-tuple-element.57) | copy-start | bytes 1540
  376.8 27.1 %copy-start.43 = (pred[4]{0:T(512)(128)(4,1)S(1)}, pred[4]{0:T(512)(128)(4,1)}, u32[]{:S(2)}) copy-start(pred[4]{0:T(512)(128)(4,1)} %get-tuple-element.55) | copy-start | bytes 16
  413.8 5.4 copy-start.27
  420.0 3.8 copy-start.29
  424.6 4.0 copy-start.17
  429.4 3.0 copy-start.19
  429.4 3.9 copy-start.8
  432.5 3.4 copy-start.21
  433.3 3.4 copy-start.10
  435.9 2.2 copy-start.25
  435.9 3.0 copy-start.13
  436.7 3.5 copy-start.34
  441.1 2.5 copy-start.6
  445.7 6.1 %copy-start.53 = (pred[512]{0:T(512)(128)(4,1)S(1)}, pred[512]{0:T(512)(128)(4,1)}, u32[]{:S(2)}) copy-start(pred[512]{0:T(512)(128)(4,1)} %broadcast_bitcast_fusion) | copy-start | bytes 1540
  451.8 3.7 copy-start.44
  464.4 6.2 %copy-start.48 = (pred[4]{0:T(512)(128)(4,1)S(1)}, pred[4]{0:T(512)(128)(4,1)}, u32[]{:S(2)}) copy-start(pred[4]{0:T(512)(128)(4,1)} %copy-done.47) | copy-start | bytes 16
  464.4 6.3 %copy-start.15 = (f32[128,4,128]{2,1,0:T(4,128)S(1)}, f32[128,4,128]{2,1,0:T(4,128)}, u32[]{:S(2)}) copy-start(f32[128,4,128]{2,1,0:T(4,128)} %broadcast_select_fusion) | copy-start | bytes 786436
  464.4 6.3 %copy-start.40 = (s32[8]{0:T(128)S(1)}, s32[8]{0:T(128)}, u32[]{:S(2)}) copy-start(s32[8]{0:T(128)} %copy-done.39) | copy-start | bytes 100
  464.4 6.3 %copy-start.42 = (pred[8]{0:T(512)(128)(4,1)S(1)}, pred[8]{0:T(512)(128)(4,1)}, u32[]{:S(2)}) copy-start(pred[8]{0:T(512)(128)(4,1)} %copy-done.41) | copy-start | bytes 28
  464.5 6.3 %copy-start.46 = (pred[8]{0:T(512)(128)(4,1)S(1)}, pred[8]{0:T(512)(128)(4,1)}, u32[]{:S(2)}) copy-start(pred[8]{0:T(512)(128)(4,1)} %copy-done.45) | copy-start | bytes 28
  480.9 7.7 %copy-start.52 = (s32[2,56]{1,0:T(2,128)S(1)}, s32[2,56]{1,0:T(2,128)}, u32[]{:S(2)}) copy-start(s32[2,56]{1,0:T(2,128)} %param.9) | copy-start | bytes 1348
  480.9 8.4 %copy-start.23 = (f32[128,128]{1,0:T(8,128)S(1)}, f32[128,128]{1,0:T(8,128)}, u32[]{:S(2)}) copy-start(f32[128,128]{1,0:T(8,128)} %copy-done.22) | copy-start | bytes 196612
  480.9 100.3 %all-to-all-start.1 = ((f32[16,1,65536]{2,1,0:T(1,128)}), f32[16,1,65536]{2,1,0:T(1,128)}, u32[]{:S(2)}, u32[]{:S(2)}) async-start(f32[16,1,65536]{2,1,0:T(1,128)} %copy.139), calls=%async_computation.1 | async-start | bytes 8388608 | tf_op jit(solution)/shard_map/all_to_all | solution.py:167
  588.9 3.1 copy-start.14
  (13 other events, 11.6 us)
Sparse Core Ops, SparseCore 0:
  11.0 50.0 all-gather.6
  173.2 32.6 all-gather.10
  208.4 73.2 all-gather.8
